TPU v7x, 128 devices: a whole 4x4x4 slice. The times are simulated.
128 devices in a mesh: ind: 32 (over z_hi, x, y), win: 4 (over z_lo, core).
Axes of the slice: x: 4, y: 4, z: 4 (z_hi: 2, z_lo: 2; z = z_hi * 2 + z_lo), core: 2. Of those that a mesh axis runs over, the one named last changes fastest.
Arguments:
- dosage: bfloat16 [65536, 4096], P('ind', 'win'), may hold values from 0 to 2
- tail: bfloat16 [65536, 512], P('ind'), may hold values from 0 to 2
- missing: int32 [4608], replicated, may hold values from 0 to 32767
- start: float32 [8, 1024, 8], P('win'), may hold values from -6 to 6
Outputs:
- loadings: float32 [8, 1024, 8], P('win')
- variances: float32 [8, 8], P('win')
- scores: float32 [65536, 8], P('ind', 'win')
All inputs are finite; a program needn't handle non-finite values.
Results may differ from a plain program's by a relative error of at most 0.0024.
Values may be sent and summed in bfloat16 or wider, within the bound.
No kernel may reach another device: no remote copies, remote signals or barrier semaphores. Data moves between devices by JAX's collectives and lax.ppermute only.
A program may use at most 128 MiB of HBM per device.

v0:
```python
import jax
import jax.numpy as jnp
from jax import lax
from jax.sharding import PartitionSpec as P

ITERS = 6


def passed_along(array, axis, by):
    size = lax.axis_size(axis)
    pairs = [(i, i + by) for i in range(size) if 0 <= i + by < size]
    return lax.ppermute(array, axis, pairs)


def orthonormal(image):
    gram = jnp.einsum("swk,swl->skl", image, image, precision=lax.Precision.HIGHEST)
    factor = jnp.linalg.cholesky(gram)
    solved = jax.vmap(lambda fac, rhs: jax.scipy.linalg.solve_triangular(fac, rhs, lower=True))(
        factor, jnp.swapaxes(image, 1, 2)
    )
    return jnp.swapaxes(solved, 1, 2)


def shards(dosage, tail, missing, start):
    win_count = lax.axis_size("win")
    position = lax.axis_index("win")
    columns = dosage.shape[1]
    half_cols = columns // 2
    total = dosage.shape[0] * lax.axis_size("ind")
    received = passed_along(dosage[:, :half_cols], "win", -1)
    following = jnp.where(position == win_count - 1, tail, received)
    region = jnp.concatenate([dosage, following], axis=1)
    regionf = region.astype(jnp.float32)
    col_sums, col_squares = lax.psum(
        (jnp.sum(regionf, axis=0), jnp.sum(regionf * regionf, axis=0)), "ind"
    )
    mean = col_sums / total
    var = col_squares / total - mean * mean
    miss_here = lax.dynamic_slice_in_dim(missing, position * columns, columns + half_cols)
    weight = jnp.sqrt((total - miss_here.astype(jnp.float32)) / total)
    stand = ((regionf - mean) / jnp.sqrt(var + 1e-05) * weight).astype(jnp.bfloat16)
    blocks = jnp.stack([stand[:, :columns], stand[:, half_cols:]], 0)
    basis = start
    first_part = jnp.dot(
        stand[:, :columns].T, stand[:, :columns], preferred_element_type=jnp.float32
    )
    second_part = jnp.dot(
        stand[:, half_cols:].T, stand[:, columns:], preferred_element_type=jnp.float32
    )
    first_sum, second_sum = lax.psum((first_part, second_part), "ind")
    first_sum = first_sum / total
    second_sum = second_sum / total
    upper_row = jnp.concatenate([first_sum[half_cols:, half_cols:], second_sum[:half_cols]], axis=1)
    lower_row = jnp.concatenate([second_sum[:half_cols].T, second_sum[half_cols:]], axis=1)
    cov = jnp.stack([first_sum, jnp.concatenate([upper_row, lower_row], axis=0)], 0)
    for step in range(ITERS):
        basis = orthonormal(jnp.einsum("swv,svk->swk", cov, basis, precision=lax.Precision.HIGHEST))
    image = jnp.einsum("swv,svk->swk", cov, basis, precision=lax.Precision.HIGHEST)
    variances = jnp.sum(basis * image, axis=1)
    proj = jnp.einsum(
        "snw,swk->snk",
        blocks,
        basis,
        precision=lax.Precision.HIGHEST,
        preferred_element_type=jnp.float32,
    )
    rest = blocks.astype(jnp.float32) - jnp.einsum(
        "snk,swk->snw", proj, basis, precision=lax.Precision.HIGHEST
    )
    scores = jnp.sum(rest * rest, axis=2) / columns
    return (basis, variances, jnp.transpose(scores))


def solution(mesh):
    in_specs = (P("ind", "win"), P("ind", None), P(), P("win", None, None))
    out_specs = (P("win", None, None), P("win", None), P("ind", "win"))
    return jax.shard_map(shards, mesh=mesh, in_specs=in_specs, out_specs=out_specs, check_vma=False)
```

profile of v0, /device:TPU:32, one launch (start us, length us, event | category | flops | bytes accessed | tf_op | source)
XLA Modules:
  0.0 743.4 jit_solution(10795360000378226511)
XLA Ops:
  7.2 6.5 copy.31
  13.7 3.3 slice.40
  17.1 1.9 collective-permute-start
  19.0 2.5 copy.30
  21.5 0.9 multiply_sqrt_fusion
  22.5 20.4 %collective-permute-done = bf16[2048,512]{0,1:T(8,128)(2,1)} collective-permute-done((bf16[2048,512]{0,1:T(8,128)(2,1)}, bf16[2048,512]{0,1:T(8,128)(2,1)}, u32[]{:S(2)}, u32[]{:S(2)}) %collective-permute-start) | collective-permute-done | bytes 2097184 | tf_op jit(solution)/shard_map/ppermute | solution.py:12
  42.9 1.8 broadcast_select_fusion
  44.7 3.7 convert_reduce_fusion
  48.4 183.8 %all-reduce = (f32[1536]{0:T(1024)S(1)}, f32[1536]{0:T(1024)S(1)}) all-reduce(f32[1536]{0:T(1024)S(1)} %get-tuple-element.6, f32[1536]{0:T(1024)S(1)} %get-tuple-element.5), channel_id=1, replica_groups=mesh['ind'=32,'win'=4] {'ind'}, use_global_device_ids=true, to_apply=%region_3.4 | all-reduce | flops 3072 | bytes 24576 | tf_op jit(solution)/shard_map/psum | solution.py:34
  232.2 5.5 fusion.2
  237.7 3.8 fusion.5
  241.5 6.2 fusion.7
  247.7 7.5 %slice_bitcast_fusion.1 = (bf16[1,2048,1024]{1,2,0:T(8,128)(2,1)}, bf16[1,2048,1024]{1,2,0:T(8,128)(2,1)}) fusion(bf16[2048,1536]{0,1:T(8,128)(2,1)} %copy-done.4), kind=kLoop, calls=%fused_computation.16 | loop fusion | bytes 16777216 | tf_op jit(solution)/shard_map/stack | solution.py:42
  255.2 363.0 %all-reduce.4.cloned.1.call-done = (f32[1024,512]{1,0:T(8,128)}, f32[1024,1024]{1,0:T(8,128)}) async-done(((f32[1024,512]{1,0:T(8,128)}, f32[1024,1024]{1,0:T(8,128)}), (f32[1024,512]{1,0:T(8,128)}, f32[1024,1024]{1,0:T(8,128)})) %all-reduce.4.cloned.1.call-update) | async-done | bytes 6291472 | tf_op jit(solution)/shard_map/psum | solution.py:50
  618.2 1.8 broadcast_multiply_fusion.1
  620.1 0.4 fusion.43
  620.4 1.3 copy.32
  621.8 3.3 fusion.36
  625.2 0.4 maximum_bitcast_fusion
  625.7 1.3 copy-done.1
  627.0 7.2 fusion.42
  634.5 1.4 custom-call.16
  636.2 1.3 custom-call.17
  637.5 0.3 fusion.21
  637.8 9.5 %fusion.41 = f32[2,1024,8]{1,2,0:T(8,128)S(1)} fusion(f32[2,8,1024]{2,1,0:T(8,128)S(1)} %fusion.21, f32[1,1024,1024]{2,1,0:T(8,128)} %copy-done.2, f32[1,1024,1024]{2,1,0:T(8,128)} %copy-done.1), kind=kOutput, calls=%fused_computation.86 | convolution fusion | flops 203423744 | bytes 8519680 | tf_op jit(solution)/shard_map/swv,svk->swk/dot_general | solution.py:57
  647.6 1.4 custom-call.18
  649.3 1.3 custom-call.19
  650.5 0.3 fusion.19
  650.8 9.7 %fusion.40 = f32[2,1024,8]{1,2,0:T(8,128)S(1)} fusion(f32[2,8,1024]{2,1,0:T(8,128)S(1)} %fusion.19, f32[1,1024,1024]{2,1,0:T(8,128)} %copy-done.2, f32[1,1024,1024]{2,1,0:T(8,128)} %copy-done.1), kind=kOutput, calls=%fused_computation.85 | convolution fusion | flops 203423744 | bytes 8519680 | tf_op jit(solution)/shard_map/swv,svk->swk/dot_general | solution.py:57
  660.8 1.4 custom-call.20
  662.5 1.3 custom-call.21
  663.8 0.3 fusion.17
  664.0 9.5 %fusion.39 = f32[2,1024,8]{1,2,0:T(8,128)S(1)} fusion(f32[2,8,1024]{2,1,0:T(8,128)S(1)} %fusion.17, f32[1,1024,1024]{2,1,0:T(8,128)} %copy-done.2, f32[1,1024,1024]{2,1,0:T(8,128)} %copy-done.1), kind=kOutput, calls=%fused_computation.84 | convolution fusion | flops 203423744 | bytes 8519680 | tf_op jit(solution)/shard_map/swv,svk->swk/dot_general | solution.py:57
  673.9 1.4 custom-call.22
  675.6 1.3 custom-call.23
  676.8 0.3 fusion.15
  677.1 9.5 %fusion.38 = f32[2,1024,8]{1,2,0:T(8,128)S(1)} fusion(f32[2,8,1024]{2,1,0:T(8,128)S(1)} %fusion.15, f32[1,1024,1024]{2,1,0:T(8,128)} %copy-done.2, f32[1,1024,1024]{2,1,0:T(8,128)} %copy-done.1), kind=kOutput, calls=%fused_computation.83 | convolution fusion | flops 203423744 | bytes 8519680 | tf_op jit(solution)/shard_map/swv,svk->swk/dot_general | solution.py:57
  686.9 1.4 custom-call.24
  688.6 1.3 custom-call.25
  689.9 0.3 fusion.13
  690.1 9.7 %fusion.37 = f32[2,1024,8]{1,2,0:T(8,128)S(1)} fusion(f32[2,8,1024]{2,1,0:T(8,128)S(1)} %fusion.13, f32[1,1024,1024]{2,1,0:T(8,128)} %copy-done.2, f32[1,1024,1024]{2,1,0:T(8,128)} %copy-done.1), kind=kOutput, calls=%fused_computation.82 | convolution fusion | flops 203423744 | bytes 8519680 | tf_op jit(solution)/shard_map/swv,svk->swk/dot_general | solution.py:57
  700.2 1.4 custom-call.26
  701.9 1.3 custom-call.27
  703.1 0.3 fusion.11
  703.4 10.3 %fusion.10 = f32[2,8]{1,0:T(2,128)} fusion(f32[2,1024,8]{1,2,0:T(8,128)S(1)} %bitcast.125, f32[2,8,1024]{2,1,0:T(8,128)S(1)} %fusion.11, f32[1,1024,1024]{2,1,0:T(8,128)} %copy-done.2, f32[1,1024,1024]{2,1,0:T(8,128)} %copy-done.1), kind=kOutput, calls=%fused_computation.23 | convolution fusion | flops 203456496 | bytes 8519744 | tf_op jit(solution)/shard_map/swv,svk->swk/dot_general | solution.py:58
  713.7 3.5 fusion.4
  717.2 18.4 %multiply_reduce_fusion = f32[2,2048]{1,0:T(2,128)S(1)} fusion(f32[2,2048,8]{1,2,0:T(8,128)S(1)} %fusion.4, f32[2,8,1024]{2,1,0:T(8,128)S(1)} %fusion.11, bf16[1,2048,1024]{1,2,0:T(8,128)(2,1)S(1)} %copy-done.6, bf16[1,2048,1024]{1,2,0:T(8,128)(2,1)S(1)} %copy-done.5), kind=kOutput, calls=%fused_computation.3 | convolution fusion | flops 423620608 | bytes 8601600 | tf_op jit(solution)/shard_map/snk,swk->snw/dot_general | solution.py:67
  735.7 0.6 multiply_bitcast_fusion
  (61 shorter events, 3.7 us)
Async XLA Ops:
  7.2 619.9 %copy-start = (f32[2,1024,8]{1,2,0:T(8,128)S(1)}, f32[2,1024,8]{1,2,0:T(8,128)}, u32[]{:S(2)}) copy-start(f32[2,1024,8]{1,2,0:T(8,128)} %param.10) | copy-start | bytes 196612
  7.2 611.1 %all-reduce.4.cloned.1.call-start = ((), (), s32[]{:S(2)}) async-start(), calls=%async_computation | async-start | bytes 12582912 | tf_op jit(solution)/shard_map/psum | solution.py:50
  13.7 5.3 copy-start.8
  17.1 25.8 %collective-permute-start = (bf16[2048,512]{0,1:T(8,128)(2,1)}, bf16[2048,512]{0,1:T(8,128)(2,1)}, u32[]{:S(2)}, u32[]{:S(2)}) collective-permute-start(bf16[2048,512]{0,1:T(8,128)(2,1)} %slice.40), channel_id=1, source_target_pairs={{1,0},{2,1},{3,2},{5,4},{6,5},{7,6},{9,8},{10,9},{11,10},{13,12},{... | collective-permute-start | bytes 6291464 | tf_op jit(solution)/shard_map/ppermute | solution.py:12
  21.5 23.2 %copy-start.3 = (bf16[2048,1024]{0,1:T(8,128)(2,1)S(1)}, bf16[2048,1024]{0,1:T(8,128)(2,1)}, u32[]{:S(2)}) copy-start(bf16[2048,1024]{0,1:T(8,128)(2,1)} %copy.31) | copy-start | bytes 12582916
  237.7 3.8 copy-start.4
  621.8 3.4 copy-start.7
  625.1 1.9 copy-start.1
  625.7 8.5 %copy-start.2 = (f32[1,1024,1024]{2,1,0:T(8,128)}, f32[1,1024,1024]{2,1,0:T(8,128)S(1)}, u32[]{:S(2)}) copy-start(f32[1,1024,1024]{2,1,0:T(8,128)S(1)} %maximum_bitcast_fusion) | copy-start | bytes 12582916
  703.4 13.8 %copy-start.9 = (f32[2,8,1024]{2,1,0:T(8,128)}, f32[2,8,1024]{2,1,0:T(8,128)S(1)}, u32[]{:S(2)}) copy-start(f32[2,8,1024]{2,1,0:T(8,128)S(1)} %fusion.11) | copy-start | bytes 196612
  703.4 10.3 %copy-start.5 = (bf16[1,2048,1024]{1,2,0:T(8,128)(2,1)S(1)}, bf16[1,2048,1024]{1,2,0:T(8,128)(2,1)}, u32[]{:S(2)}) copy-start(bf16[1,2048,1024]{1,2,0:T(8,128)(2,1)} %get-tuple-element.11) | copy-start | bytes 12582916
  703.4 10.3 %copy-start.6 = (bf16[1,2048,1024]{1,2,0:T(8,128)(2,1)S(1)}, bf16[1,2048,1024]{1,2,0:T(8,128)(2,1)}, u32[]{:S(2)}) copy-start(bf16[1,2048,1024]{1,2,0:T(8,128)(2,1)} %get-tuple-element.12) | copy-start | bytes 12582916
Sparse Core Ops, SparseCore 0:
  247.8 370.4 all-reduce.3
where the time goes:
time: 752 us; the launch traced here: 743 us
  waiting for transfers between devices  383 us (51%)
  blocking collectives  184 us (24%)
  matrix products  100 us (13%)
  other arithmetic  35.9 us (5%)
  local copies, waits for them, and re-layouts  23.5 us (3%)
  between operations  14.6 us (2%)
    psum x1, waiting for transfers between devices, shards(): first_sum, second_sum = lax.psum((first_part, second_part), 'ind')  363 us
    psum x1, blocking collectives, shards(): lax.psum((jnp.sum(regionf, axis=0), jnp.sum(regionf * regionf, axis=0)),...  184 us
    dot_general x7, matrix products, shards(): jnp.einsum('swv,svk->swk', cov, basis, precision=lax.Precision.HIGHEST)  65.2 us
    ppermute x1, waiting for transfers between devices, passed_along(): return lax.ppermute(array, axis, pairs)  20.4 us
    dot_general x1, matrix products, shards(): jnp.einsum('snk,swk->snw', proj, basis, precision=lax.Precision.HIGHEST)  18.4 us
  transfers between devices with their start and end apart: 2, of which 2 were waited for; matrix products, arithmetic and copies ran while one was open for 1% of the time, Pallas kernels for 0%

commit v1 on v0

v1 whole, which is shorter than its diff:
```python
import jax
import jax.numpy as jnp
from jax import lax
from jax.sharding import PartitionSpec as P

ITERS = 6
HIGHEST = lax.Precision.HIGHEST


def passed_along(array, axis, by):
    size = lax.axis_size(axis)
    pairs = [(i, i + by) for i in range(size) if 0 <= i + by < size]
    return lax.ppermute(array, axis, pairs)


def swapped(value, axis, mask):
    size = lax.axis_size(axis)
    return lax.ppermute(value, axis, [(i, i ^ mask) for i in range(size)])


def summed(value, axis):
    size = lax.axis_size(axis)
    if size & (size - 1):
        return lax.psum(value, axis)
    bit = 1
    while bit < size:
        if bit * 4 <= size:
            near = swapped(value, axis, bit)
            mid = swapped(value, axis, 2 * bit)
            far = swapped(value, axis, 3 * bit)
            value = (value + near) + (mid + far)
            bit *= 4
        else:
            value = value + swapped(value, axis, bit)
            bit *= 2
    return value


def orthonormal(image):
    gram = jnp.einsum("swk,swl->skl", image, image, precision=HIGHEST)
    factor = jnp.linalg.cholesky(gram)
    solved = jax.vmap(lambda fac, rhs: jax.scipy.linalg.solve_triangular(fac, rhs, lower=True))(
        factor, jnp.swapaxes(image, 1, 2)
    )
    return jnp.swapaxes(solved, 1, 2)


def widened(basis, half_cols):
    pad = jnp.zeros((half_cols, basis.shape[2]), basis.dtype)
    first = jnp.concatenate([basis[0], pad], axis=0)
    second = jnp.concatenate([pad, basis[1]], axis=0)
    return jnp.concatenate([first, second], axis=1)


def shards(dosage, tail, missing, start):
    win_count = lax.axis_size("win")
    position = lax.axis_index("win")
    columns = dosage.shape[1]
    half_cols = columns // 2
    comps = start.shape[2]
    total = dosage.shape[0] * lax.axis_size("ind")
    received = passed_along(dosage[:, :half_cols], "win", -1)
    following = jnp.where(position == win_count - 1, tail, received)
    region = jnp.concatenate([dosage, following], axis=1)
    regionf = region.astype(jnp.float32)
    stats = summed(jnp.stack([jnp.sum(regionf, axis=0), jnp.sum(regionf * regionf, axis=0)]), "ind")
    mean = stats[0] / total
    var = stats[1] / total - mean * mean
    miss_here = lax.dynamic_slice_in_dim(missing, position * columns, columns + half_cols)
    weight = jnp.sqrt((total - miss_here.astype(jnp.float32)) / total)
    stand = ((regionf - mean) / jnp.sqrt(var + 1e-05) * weight).astype(jnp.bfloat16)
    standf = stand.astype(jnp.float32)

    def project(basis):
        return jnp.dot(standf, widened(basis, half_cols), precision=HIGHEST)

    def image_of(basis):
        proj = project(basis)
        back = lax.dot_general(standf, proj, (((0,), (0,)), ((), ())), precision=HIGHEST)
        parts = jnp.stack([back[:columns, :comps], back[half_cols:, comps:]], 0)
        return summed(parts, "ind") / total

    basis = start
    for step in range(ITERS):
        basis = orthonormal(image_of(basis))
    proj = project(basis)
    variances = summed(jnp.sum(proj * proj, axis=0), "ind").reshape(2, comps) / total
    first = standf[:, :columns] - jnp.dot(proj[:, :comps], basis[0].T, precision=HIGHEST)
    second = standf[:, half_cols:] - jnp.dot(proj[:, comps:], basis[1].T, precision=HIGHEST)
    scores = jnp.stack([jnp.sum(first * first, axis=1), jnp.sum(second * second, axis=1)], 1) / columns
    return (basis, variances, scores)


def solution(mesh):
    in_specs = (P("ind", "win"), P("ind", None), P(), P("win", None, None))
    out_specs = (P("win", None, None), P("win", None), P("ind", "win"))
    return jax.shard_map(shards, mesh=mesh, in_specs=in_specs, out_specs=out_specs, check_vma=False)
```

time: 752 us -> 372 us (0.49)
  waiting for transfers between devices: 383 us -> 100 us
  blocking collectives: 184 us -> 0 us
  starting transfers between devices: 1.95 us -> 105 us
  matrix products: 100 us -> 114 us
  between operations: 14.6 us -> 1.8 us
  local copies, waits for them, and re-layouts: 23.5 us -> 13.6 us
    psum x1 -> x0, waiting for transfers between devices: 363 us -> none  [shards(): first_sum, second_sum = lax.psum((first_part, second_part), 'ind')]
    psum x1 -> x0, blocking collectives: 184 us -> none  [shards(): lax.psum((jnp.sum(regionf, axis=0), jnp.sum(regionf * regionf, axis=0)),...]
    ppermute x0 -> x56, starting transfers between devices: none -> 103 us  [swapped(): return lax.ppermute(value, axis, [(i, i ^ mask) for i in range(size)])]
    ppermute x0 -> x56, waiting for transfers between devices: none -> 78.7 us  [swapped(): return lax.ppermute(value, axis, [(i, i ^ mask) for i in range(size)])]
    dot_general x17 -> x21, matrix products: 98.5 us -> 112 us  [the longest x7 55.6 us: project(): return jnp.dot(standf, widened(basis, half_cols), precision=HIGHEST)]
  transfers between devices with their start and end apart: 2 -> 57, of which waited for: 2 -> 42; matrix products, arithmetic and copies ran while one was open for 1% -> 1% of each run, Pallas kernels for 0% -> 0%
where the time goes in v1:
time: 372 us; the launch traced here: 368 us
  matrix products  114 us (31%)
  starting transfers between devices  105 us (28%)
  waiting for transfers between devices  100 us (27%)
  other arithmetic  33.2 us (9%)
  local copies, waits for them, and re-layouts  13.6 us (4%)
    ppermute x56, starting transfers between devices, swapped(): return lax.ppermute(value, axis, [(i, i ^ mask) for i in range(size)])  103 us
    ppermute x56, waiting for transfers between devices, swapped(): return lax.ppermute(value, axis, [(i, i ^ mask) for i in range(size)])  78.7 us
    dot_general x7, matrix products, project(): return jnp.dot(standf, widened(basis, half_cols), precision=HIGHEST)  55.6 us
    dot_general x6, matrix products, image_of(): lax.dot_general(standf, proj, (((0,), (0,)), ((), ())), precision=HIGHEST)  38.5 us
    ppermute x1, waiting for transfers between devices, passed_along(): return lax.ppermute(array, axis, pairs)  21.4 us
    another operation x19, other arithmetic, orthonormal(): factor = jnp.linalg.cholesky(gram)  9.73 us
    dot_general x1, matrix products, shards(): jnp.dot(proj[:, :comps], basis[0].T, precision=HIGHEST)  9.48 us
    unnamed x20, local copies, waits for them, and re-layouts  9.22 us
  transfers between devices with their start and end apart: 57, of which 42 were waited for; matrix products, arithmetic and copies ran while one was open for 1% of the time, Pallas kernels for 0%

profile of v1, /device:TPU:32, one launch (start us, length us, event | category | flops | bytes accessed | tf_op | source)
XLA Modules:
  0.0 368.0 jit_solution(10293195906122908646)
XLA Ops:
  0.6 6.7 %copy.30 = bf16[2048,1024]{0,1:T(8,128)(2,1)} copy(bf16[2048,1024]{1,0:T(8,128)(2,1)} %param.7) | data formatting | bytes 8388608 | tf_op args[0]
  7.3 3.1 slice.142
  14.9 21.4 %collective-permute-done = bf16[2048,512]{0,1:T(8,128)(2,1)} collective-permute-done((bf16[2048,512]{0,1:T(8,128)(2,1)}, bf16[2048,512]{0,1:T(8,128)(2,1)}, u32[]{:S(2)}, u32[]{:S(2)}) %collective-permute-start) | collective-permute-done | bytes 2097184 | tf_op jit(solution)/shard_map/ppermute | solution.py:13
  38.1 3.7 convert_reduce_fusion
  43.5 2.9 collective-permute-start.2
  52.9 2.7 collective-permute-start.5
  60.5 3.4 collective-permute-start.7
  66.1 8.2 %fusion.126 = (f32[2048,1536]{0,1:T(8,128)}, bf16[2048,1536]{0,1:T(8,128)(2,1)S(1)}) fusion(f32[1536]{0:T(1024)S(1)} %multiply_sqrt_fusion, f32[1536]{0:T(1024)S(1)} %get-tuple-element.8, f32[1536]{0:T(1024)S(1)} %get-tuple-element.7, bf16[2048,512]{0,1:T(8,128)(2,1)S(1)} %broadcast_select_fusion, bf16[2048,1024]{0,1:T(8,128)(2,1)} %copy.30), kind=kLoop, calls=%fused_computation.226 | loop fusion | flops 28311552 | bytes 25184256 | tf_op jit(solution)/shard_map/convert_element_type | solution.py:72
  74.3 7.0 %fusion.33 = f32[2048,16]{1,0:T(8,128)S(1)} fusion(bf16[2048,1536]{0,1:T(8,128)(2,1)S(1)} %get-tuple-element.10, f32[1024,8]{0,1:T(8,128)S(1)} %get-tuple-element.36, f32[1024,8]{0,1:T(8,128)S(1)} %get-tuple-element.35), kind=kOutput, calls=%fused_computation.46 | convolution fusion | flops 604102656 | bytes 6488064 | tf_op jit(solution)/shard_map/dot_general | solution.py:75
  81.3 5.0 %fusion.128 = f32[1536,16]{0,1:T(8,128)S(1)} fusion(bf16[2048,1536]{0,1:T(8,128)(2,1)S(1)} %get-tuple-element.10, f32[2048,16]{1,0:T(8,128)S(1)} %fusion.33), kind=kOutput, calls=%fused_computation.227 | convolution fusion | flops 603979776 | bytes 6520832 | tf_op jit(solution)/shard_map/dot_general | solution.py:79
  86.7 4.4 %collective-permute-start.9 = (f32[2,1024,8]{1,2,0:T(8,128)S(1)}, f32[2,1024,8]{1,2,0:T(8,128)S(1)}, u32[]{:S(2)}, u32[]{:S(2)}) collective-permute-start(f32[2,1024,8]{1,2,0:T(8,128)S(1)} %pad_maximum_fusion.1), channel_id=1, source_target_pairs={{0,8},{4,12},{8,0},{12,4},{16,24},{20,28},{24,16},{28,20},{32,40},... | collective-permute-start | bytes 196616 | tf_op jit(solution)/shard_map/ppermute | solution.py:18
  96.3 2.8 collective-permute-start.13
  101.8 3.1 collective-permute-start.14
  105.0 2.7 collective-permute-done.14
  111.3 8.9 %fusion.30 = f32[2048,16]{1,0:T(8,128)S(1)} fusion(bf16[2048,1536]{0,1:T(8,128)(2,1)} %copy-done, f32[1024,8]{0,1:T(8,128)S(1)} %get-tuple-element.34, f32[1024,8]{0,1:T(8,128)S(1)} %get-tuple-element.33), kind=kOutput, calls=%fused_computation.44 | convolution fusion | flops 604102656 | bytes 6488064 | tf_op jit(solution)/shard_map/dot_general | solution.py:75
  120.1 5.0 %fusion.129 = f32[1536,16]{0,1:T(8,128)S(1)} fusion(bf16[2048,1536]{0,1:T(8,128)(2,1)S(1)} %copy-done.1, f32[2048,16]{1,0:T(8,128)S(1)} %fusion.30), kind=kOutput, calls=%fused_computation.228 | convolution fusion | flops 603979776 | bytes 6520832 | tf_op jit(solution)/shard_map/dot_general | solution.py:79
  134.1 3.8 %collective-permute-start.19 = (f32[2,1024,8]{1,2,0:T(8,128)S(1)}, f32[2,1024,8]{1,2,0:T(8,128)S(1)}, u32[]{:S(2)}, u32[]{:S(2)}) collective-permute-start(f32[2,1024,8]{1,2,0:T(8,128)S(1)} %add_add_fusion.9), channel_id=1, source_target_pairs={{0,32},{4,36},{8,40},{12,44},{16,48},{20,52},{24,56},{28,60},{32,0... | collective-permute-start | bytes 196616 | tf_op jit(solution)/shard_map/ppermute | solution.py:18
  143.5 3.7 %collective-permute-start.21 = (f32[2,1024,8]{1,2,0:T(8,128)S(1)}, f32[2,1024,8]{1,2,0:T(8,128)S(1)}, u32[]{:S(2)}, u32[]{:S(2)}) collective-permute-start(f32[2,1024,8]{1,2,0:T(8,128)S(1)} %add_add_fusion.8), channel_id=1, source_target_pairs={{0,64},{4,68},{8,72},{12,76},{16,80},{20,84},{24,88},{28,92},{32,9... | collective-permute-start | bytes 196616 | tf_op jit(solution)/shard_map/ppermute | solution.py:18
  153.4 8.7 %fusion.27 = f32[2048,16]{1,0:T(8,128)S(1)} fusion(bf16[2048,1536]{0,1:T(8,128)(2,1)} %copy-done, f32[1024,8]{0,1:T(8,128)S(1)} %get-tuple-element.32, f32[1024,8]{0,1:T(8,128)S(1)} %get-tuple-element.31), kind=kOutput, calls=%fused_computation.42 | convolution fusion | flops 604102656 | bytes 6488064 | tf_op jit(solution)/shard_map/dot_general | solution.py:75
  162.1 7.1 %fusion.130 = f32[1536,16]{0,1:T(8,128)S(1)} fusion(bf16[2048,1536]{0,1:T(8,128)(2,1)} %copy-done, f32[2048,16]{1,0:T(8,128)S(1)} %fusion.27), kind=kOutput, calls=%fused_computation.229 | convolution fusion | flops 603979776 | bytes 6520832 | tf_op jit(solution)/shard_map/dot_general | solution.py:79
  169.5 3.1 collective-permute-start.23
  180.1 2.8 collective-permute-start.27
  185.6 3.3 collective-permute-start.28
  188.9 2.7 collective-permute-done.28
  195.2 8.7 %fusion.24 = f32[2048,16]{1,0:T(8,128)S(1)} fusion(bf16[2048,1536]{0,1:T(8,128)(2,1)} %copy-done, f32[1024,8]{0,1:T(8,128)S(1)} %get-tuple-element.30, f32[1024,8]{0,1:T(8,128)S(1)} %get-tuple-element.29), kind=kOutput, calls=%fused_computation.40 | convolution fusion | flops 604102656 | bytes 6488064 | tf_op jit(solution)/shard_map/dot_general | solution.py:75
  203.9 7.1 %fusion.131 = f32[1536,16]{0,1:T(8,128)S(1)} fusion(bf16[2048,1536]{0,1:T(8,128)(2,1)} %copy-done, f32[2048,16]{1,0:T(8,128)S(1)} %fusion.24), kind=kOutput, calls=%fused_computation.230 | convolution fusion | flops 603979776 | bytes 6520832 | tf_op jit(solution)/shard_map/dot_general | solution.py:79
  211.2 2.9 collective-permute-start.30
  217.0 2.8 collective-permute-done.31
  220.6 3.4 collective-permute-start.33
  229.5 3.4 collective-permute-start.35
  232.9 2.7 collective-permute-done.35
  239.1 8.7 %fusion.21 = f32[2048,16]{1,0:T(8,128)S(1)} fusion(bf16[2048,1536]{0,1:T(8,128)(2,1)} %copy-done, f32[1024,8]{0,1:T(8,128)S(1)} %get-tuple-element.28, f32[1024,8]{0,1:T(8,128)S(1)} %get-tuple-element.27), kind=kOutput, calls=%fused_computation.38 | convolution fusion | flops 604102656 | bytes 6488064 | tf_op jit(solution)/shard_map/dot_general | solution.py:75
  247.8 7.1 %fusion.132 = f32[1536,16]{0,1:T(8,128)S(1)} fusion(bf16[2048,1536]{0,1:T(8,128)(2,1)} %copy-done, f32[2048,16]{1,0:T(8,128)S(1)} %fusion.21), kind=kOutput, calls=%fused_computation.231 | convolution fusion | flops 603979776 | bytes 6520832 | tf_op jit(solution)/shard_map/dot_general | solution.py:79
  255.1 3.2 collective-permute-start.37
  271.5 3.4 collective-permute-start.42
  274.9 2.7 collective-permute-done.42
  281.2 8.7 %fusion.12 = f32[2048,16]{1,0:T(8,128)S(1)} fusion(bf16[2048,1536]{0,1:T(8,128)(2,1)} %copy-done, f32[1024,8]{0,1:T(8,128)S(1)} %get-tuple-element.26, f32[1024,8]{0,1:T(8,128)S(1)} %get-tuple-element.25), kind=kOutput, calls=%fused_computation.28 | convolution fusion | flops 604102656 | bytes 6488064 | tf_op jit(solution)/shard_map/dot_general | solution.py:75
  289.9 7.1 %fusion.133 = f32[1536,16]{0,1:T(8,128)S(1)} fusion(bf16[2048,1536]{0,1:T(8,128)(2,1)} %copy-done, f32[2048,16]{1,0:T(8,128)S(1)} %fusion.12), kind=kOutput, calls=%fused_computation.232 | convolution fusion | flops 603979776 | bytes 6520832 | tf_op jit(solution)/shard_map/dot_general | solution.py:79
  297.2 3.1 collective-permute-start.44
  306.0 3.8 %collective-permute-start.47 = (f32[2,1024,8]{1,2,0:T(8,128)S(1)}, f32[2,1024,8]{1,2,0:T(8,128)S(1)}, u32[]{:S(2)}, u32[]{:S(2)}) collective-permute-start(f32[2,1024,8]{1,2,0:T(8,128)S(1)} %add_add_fusion.1), channel_id=1, source_target_pairs={{0,32},{4,36},{8,40},{12,44},{16,48},{20,52},{24,56},{28,60},{32,0... | collective-permute-start | bytes 196616 | tf_op jit(solution)/shard_map/ppermute | solution.py:18
  315.2 3.5 collective-permute-start.49
  318.7 2.7 collective-permute-done.49
  325.0 4.8 %multiply_reduce_fusion = (f32[16]{0:T(128)S(1)}, f32[2048,16]{0,1:T(8,128)S(1)}) fusion(bf16[2048,1536]{0,1:T(8,128)(2,1)} %copy-done, f32[1024,8]{0,1:T(8,128)S(1)} %get-tuple-element.24, f32[1024,8]{0,1:T(8,128)S(1)} %get-tuple-element.23), kind=kOutput, calls=%fused_computation.21 | convolution fusion | flops 604168192 | bytes 6488128 | tf_op jit(solution)/shard_map/dot_general | solution.py:75
  329.8 9.5 %fusion.7 = f32[2048]{0:T(1024)S(1)} fusion(f32[2048,1536]{0,1:T(8,128)} %get-tuple-element.9, f32[2048,16]{0,1:T(8,128)S(1)} %get-tuple-element.38, f32[2,1024,8]{1,2,0:T(8,128)S(1)} %convolution_bitcast_fusion), kind=kOutput, calls=%fused_computation.12 | convolution fusion | flops 207616000 | bytes 8495104 | tf_op jit(solution)/shard_map/dot_general | solution.py:88
  339.4 7.4 %fusion.5 = f32[2048]{0:T(1024)S(1)} fusion(f32[2048,1536]{0,1:T(8,128)S(1)} %bitcast.178, f32[2048,16]{0,1:T(8,128)S(1)} %get-tuple-element.38, f32[2,1024,8]{1,2,0:T(8,128)S(1)} %convolution_bitcast_fusion), kind=kOutput, calls=%fused_computation.9 | convolution fusion | flops 207616000 | bytes 8495104 | tf_op jit(solution)/shard_map/dot_general | solution.py:89
  346.9 3.2 collective-permute-start.51
  352.0 2.8 collective-permute-done.52
  361.8 3.0 collective-permute-start.56
  (206 shorter events, 124.1 us)
Async XLA Ops:
  10.5 25.8 %collective-permute-start = (bf16[2048,512]{0,1:T(8,128)(2,1)}, bf16[2048,512]{0,1:T(8,128)(2,1)}, u32[]{:S(2)}, u32[]{:S(2)}) collective-permute-start(bf16[2048,512]{0,1:T(8,128)(2,1)} %slice.142), channel_id=1, source_target_pairs={{1,0},{2,1},{3,2},{5,4},{6,5},{7,6},{9,8},{10,9},{11,10},{13,12},{... | collective-permute-start | bytes 6291464 | tf_op jit(solution)/shard_map/ppermute | solution.py:13
  41.8 4.8 %collective-permute-start.1 = (f32[2,1536]{1,0:T(2,128)S(1)}, f32[2,1536]{1,0:T(2,128)S(1)}, u32[]{:S(2)}, u32[]{:S(2)}) collective-permute-start(f32[2,1536]{1,0:T(2,128)S(1)} %pad_maximum_fusion.7), channel_id=1, source_target_pairs={{0,4},{4,0},{8,12},{12,8},{16,20},{20,16},{24,28},{28,24},{32,36},... | collective-permute-start | bytes 36872 | tf_op jit(solution)/shard_map/ppermute | solution.py:18
  43.5 5.2 %collective-permute-start.2 = (f32[2,1536]{1,0:T(2,128)S(1)}, f32[2,1536]{1,0:T(2,128)S(1)}, u32[]{:S(2)}, u32[]{:S(2)}) collective-permute-start(f32[2,1536]{1,0:T(2,128)S(1)} %pad_maximum_fusion.7), channel_id=1, source_target_pairs={{0,8},{4,12},{8,0},{12,4},{16,24},{20,28},{24,16},{28,20},{32,40},... | collective-permute-start | bytes 36872 | tf_op jit(solution)/shard_map/ppermute | solution.py:18
  46.4 4.9 %collective-permute-start.3 = (f32[2,1536]{1,0:T(2,128)S(1)}, f32[2,1536]{1,0:T(2,128)S(1)}, u32[]{:S(2)}, u32[]{:S(2)}) collective-permute-start(f32[2,1536]{1,0:T(2,128)S(1)} %pad_maximum_fusion.7), channel_id=1, source_target_pairs={{0,12},{4,8},{8,4},{12,0},{16,28},{20,24},{24,20},{28,16},{32,44},... | collective-permute-start | bytes 36872 | tf_op jit(solution)/shard_map/ppermute | solution.py:18
  51.3 4.8 %collective-permute-start.4 = (f32[2,1536]{1,0:T(2,128)S(1)}, f32[2,1536]{1,0:T(2,128)S(1)}, u32[]{:S(2)}, u32[]{:S(2)}) collective-permute-start(f32[2,1536]{1,0:T(2,128)S(1)} %add_add_fusion.13), channel_id=1, source_target_pairs={{0,16},{4,20},{8,24},{12,28},{16,0},{20,4},{24,8},{28,12},{32,48},... | collective-permute-start | bytes 36872 | tf_op jit(solution)/shard_map/ppermute | solution.py:18
  52.9 5.2 %collective-permute-start.5 = (f32[2,1536]{1,0:T(2,128)S(1)}, f32[2,1536]{1,0:T(2,128)S(1)}, u32[]{:S(2)}, u32[]{:S(2)}) collective-permute-start(f32[2,1536]{1,0:T(2,128)S(1)} %add_add_fusion.13), channel_id=1, source_target_pairs={{0,32},{4,36},{8,40},{12,44},{16,48},{20,52},{24,56},{28,60},{32,0... | collective-permute-start | bytes 36872 | tf_op jit(solution)/shard_map/ppermute | solution.py:18
  55.6 4.9 %collective-permute-start.6 = (f32[2,1536]{1,0:T(2,128)S(1)}, f32[2,1536]{1,0:T(2,128)S(1)}, u32[]{:S(2)}, u32[]{:S(2)}) collective-permute-start(f32[2,1536]{1,0:T(2,128)S(1)} %add_add_fusion.13), channel_id=1, source_target_pairs={{0,48},{4,52},{8,56},{12,60},{16,32},{20,36},{24,40},{28,44},{32,1... | collective-permute-start | bytes 36872 | tf_op jit(solution)/shard_map/ppermute | solution.py:18
  60.5 5.5 %collective-permute-start.7 = (f32[2,1536]{1,0:T(2,128)S(1)}, f32[2,1536]{1,0:T(2,128)S(1)}, u32[]{:S(2)}, u32[]{:S(2)}) collective-permute-start(f32[2,1536]{1,0:T(2,128)S(1)} %add_add_fusion.12), channel_id=1, source_target_pairs={{0,64},{4,68},{8,72},{12,76},{16,80},{20,84},{24,88},{28,92},{32,9... | collective-permute-start | bytes 36872 | tf_op jit(solution)/shard_map/ppermute | solution.py:18
  86.3 5.6 %collective-permute-start.10 = (f32[2,1024,8]{1,2,0:T(8,128)S(1)}, f32[2,1024,8]{1,2,0:T(8,128)S(1)}, u32[]{:S(2)}, u32[]{:S(2)}) collective-permute-start(f32[2,1024,8]{1,2,0:T(8,128)S(1)} %pad_maximum_fusion.1), channel_id=1, source_target_pairs={{0,12},{4,8},{8,4},{12,0},{16,28},{20,24},{24,20},{28,16},{32,44},... | collective-permute-start | bytes 196616 | tf_op jit(solution)/shard_map/ppermute | solution.py:18
  86.6 5.3 %collective-permute-start.8 = (f32[2,1024,8]{1,2,0:T(8,128)S(1)}, f32[2,1024,8]{1,2,0:T(8,128)S(1)}, u32[]{:S(2)}, u32[]{:S(2)}) collective-permute-start(f32[2,1024,8]{1,2,0:T(8,128)S(1)} %pad_maximum_fusion.1), channel_id=1, source_target_pairs={{0,4},{4,0},{8,12},{12,8},{16,20},{20,16},{24,28},{28,24},{32,36},... | collective-permute-start | bytes 196616 | tf_op jit(solution)/shard_map/ppermute | solution.py:18
  86.7 7.4 %collective-permute-start.9 = (f32[2,1024,8]{1,2,0:T(8,128)S(1)}, f32[2,1024,8]{1,2,0:T(8,128)S(1)}, u32[]{:S(2)}, u32[]{:S(2)}) collective-permute-start(f32[2,1024,8]{1,2,0:T(8,128)S(1)} %pad_maximum_fusion.1), channel_id=1, source_target_pairs={{0,8},{4,12},{8,0},{12,4},{16,24},{20,28},{24,16},{28,20},{32,40},... | collective-permute-start | bytes 196616 | tf_op jit(solution)/shard_map/ppermute | solution.py:18
  94.1 5.0 %collective-permute-start.11 = (f32[2,1024,8]{1,2,0:T(8,128)S(1)}, f32[2,1024,8]{1,2,0:T(8,128)S(1)}, u32[]{:S(2)}, u32[]{:S(2)}) collective-permute-start(f32[2,1024,8]{1,2,0:T(8,128)S(1)} %add_add_fusion.11), channel_id=1, source_target_pairs={{0,16},{4,20},{8,24},{12,28},{16,0},{20,4},{24,8},{28,12},{32,48},... | collective-permute-start | bytes 196616 | tf_op jit(solution)/shard_map/ppermute | solution.py:18
  94.2 6.1 %collective-permute-start.12 = (f32[2,1024,8]{1,2,0:T(8,128)S(1)}, f32[2,1024,8]{1,2,0:T(8,128)S(1)}, u32[]{:S(2)}, u32[]{:S(2)}) collective-permute-start(f32[2,1024,8]{1,2,0:T(8,128)S(1)} %add_add_fusion.11), channel_id=1, source_target_pairs={{0,32},{4,36},{8,40},{12,44},{16,48},{20,52},{24,56},{28,60},{32,0... | collective-permute-start | bytes 196616 | tf_op jit(solution)/shard_map/ppermute | solution.py:18
  96.3 5.5 %collective-permute-start.13 = (f32[2,1024,8]{1,2,0:T(8,128)S(1)}, f32[2,1024,8]{1,2,0:T(8,128)S(1)}, u32[]{:S(2)}, u32[]{:S(2)}) collective-permute-start(f32[2,1024,8]{1,2,0:T(8,128)S(1)} %add_add_fusion.11), channel_id=1, source_target_pairs={{0,48},{4,52},{8,56},{12,60},{16,32},{20,36},{24,40},{28,44},{32,1... | collective-permute-start | bytes 196616 | tf_op jit(solution)/shard_map/ppermute | solution.py:18
  101.8 5.8 %collective-permute-start.14 = (f32[2,1024,8]{1,2,0:T(8,128)S(1)}, f32[2,1024,8]{1,2,0:T(8,128)S(1)}, u32[]{:S(2)}, u32[]{:S(2)}) collective-permute-start(f32[2,1024,8]{1,2,0:T(8,128)S(1)} %add_add_fusion.10), channel_id=1, source_target_pairs={{0,64},{4,68},{8,72},{12,76},{16,80},{20,84},{24,88},{28,92},{32,9... | collective-permute-start | bytes 196616 | tf_op jit(solution)/shard_map/ppermute | solution.py:18
  125.2 4.8 %collective-permute-start.15 = (f32[2,1024,8]{1,2,0:T(8,128)S(1)}, f32[2,1024,8]{1,2,0:T(8,128)S(1)}, u32[]{:S(2)}, u32[]{:S(2)}) collective-permute-start(f32[2,1024,8]{1,2,0:T(8,128)S(1)} %pad_maximum_fusion.2), channel_id=1, source_target_pairs={{0,4},{4,0},{8,12},{12,8},{16,20},{20,16},{24,28},{28,24},{32,36},... | collective-permute-start | bytes 196616 | tf_op jit(solution)/shard_map/ppermute | solution.py:18
  125.6 5.8 %collective-permute-start.16 = (f32[2,1024,8]{1,2,0:T(8,128)S(1)}, f32[2,1024,8]{1,2,0:T(8,128)S(1)}, u32[]{:S(2)}, u32[]{:S(2)}) collective-permute-start(f32[2,1024,8]{1,2,0:T(8,128)S(1)} %pad_maximum_fusion.2), channel_id=1, source_target_pairs={{0,8},{4,12},{8,0},{12,4},{16,24},{20,28},{24,16},{28,20},{32,40},... | collective-permute-start | bytes 196616 | tf_op jit(solution)/shard_map/ppermute | solution.py:18
  128.2 5.5 %collective-permute-start.17 = (f32[2,1024,8]{1,2,0:T(8,128)S(1)}, f32[2,1024,8]{1,2,0:T(8,128)S(1)}, u32[]{:S(2)}, u32[]{:S(2)}) collective-permute-start(f32[2,1024,8]{1,2,0:T(8,128)S(1)} %pad_maximum_fusion.2), channel_id=1, source_target_pairs={{0,12},{4,8},{8,4},{12,0},{16,28},{20,24},{24,20},{28,16},{32,44},... | collective-permute-start | bytes 196616 | tf_op jit(solution)/shard_map/ppermute | solution.py:18
  133.7 4.8 %collective-permute-start.18 = (f32[2,1024,8]{1,2,0:T(8,128)S(1)}, f32[2,1024,8]{1,2,0:T(8,128)S(1)}, u32[]{:S(2)}, u32[]{:S(2)}) collective-permute-start(f32[2,1024,8]{1,2,0:T(8,128)S(1)} %add_add_fusion.9), channel_id=1, source_target_pairs={{0,16},{4,20},{8,24},{12,28},{16,0},{20,4},{24,8},{28,12},{32,48},... | collective-permute-start | bytes 196616 | tf_op jit(solution)/shard_map/ppermute | solution.py:18
  134.1 6.8 %collective-permute-start.19 = (f32[2,1024,8]{1,2,0:T(8,128)S(1)}, f32[2,1024,8]{1,2,0:T(8,128)S(1)}, u32[]{:S(2)}, u32[]{:S(2)}) collective-permute-start(f32[2,1024,8]{1,2,0:T(8,128)S(1)} %add_add_fusion.9), channel_id=1, source_target_pairs={{0,32},{4,36},{8,40},{12,44},{16,48},{20,52},{24,56},{28,60},{32,0... | collective-permute-start | bytes 196616 | tf_op jit(solution)/shard_map/ppermute | solution.py:18
  138.0 5.5 %collective-permute-start.20 = (f32[2,1024,8]{1,2,0:T(8,128)S(1)}, f32[2,1024,8]{1,2,0:T(8,128)S(1)}, u32[]{:S(2)}, u32[]{:S(2)}) collective-permute-start(f32[2,1024,8]{1,2,0:T(8,128)S(1)} %add_add_fusion.9), channel_id=1, source_target_pairs={{0,48},{4,52},{8,56},{12,60},{16,32},{20,36},{24,40},{28,44},{32,1... | collective-permute-start | bytes 196616 | tf_op jit(solution)/shard_map/ppermute | solution.py:18
  143.5 6.3 %collective-permute-start.21 = (f32[2,1024,8]{1,2,0:T(8,128)S(1)}, f32[2,1024,8]{1,2,0:T(8,128)S(1)}, u32[]{:S(2)}, u32[]{:S(2)}) collective-permute-start(f32[2,1024,8]{1,2,0:T(8,128)S(1)} %add_add_fusion.8), channel_id=1, source_target_pairs={{0,64},{4,68},{8,72},{12,76},{16,80},{20,84},{24,88},{28,92},{32,9... | collective-permute-start | bytes 196616 | tf_op jit(solution)/shard_map/ppermute | solution.py:18
  169.3 4.8 %collective-permute-start.22 = (f32[2,1024,8]{1,2,0:T(8,128)S(1)}, f32[2,1024,8]{1,2,0:T(8,128)S(1)}, u32[]{:S(2)}, u32[]{:S(2)}) collective-permute-start(f32[2,1024,8]{1,2,0:T(8,128)S(1)} %pad_maximum_fusion.3), channel_id=1, source_target_pairs={{0,4},{4,0},{8,12},{12,8},{16,20},{20,16},{24,28},{28,24},{32,36},... | collective-permute-start | bytes 196616 | tf_op jit(solution)/shard_map/ppermute | solution.py:18
  169.5 6.1 %collective-permute-start.23 = (f32[2,1024,8]{1,2,0:T(8,128)S(1)}, f32[2,1024,8]{1,2,0:T(8,128)S(1)}, u32[]{:S(2)}, u32[]{:S(2)}) collective-permute-start(f32[2,1024,8]{1,2,0:T(8,128)S(1)} %pad_maximum_fusion.3), channel_id=1, source_target_pairs={{0,8},{4,12},{8,0},{12,4},{16,24},{20,28},{24,16},{28,20},{32,40},... | collective-permute-start | bytes 196616 | tf_op jit(solution)/shard_map/ppermute | solution.py:18
  172.6 5.5 %collective-permute-start.24 = (f32[2,1024,8]{1,2,0:T(8,128)S(1)}, f32[2,1024,8]{1,2,0:T(8,128)S(1)}, u32[]{:S(2)}, u32[]{:S(2)}) collective-permute-start(f32[2,1024,8]{1,2,0:T(8,128)S(1)} %pad_maximum_fusion.3), channel_id=1, source_target_pairs={{0,12},{4,8},{8,4},{12,0},{16,28},{20,24},{24,20},{28,16},{32,44},... | collective-permute-start | bytes 196616 | tf_op jit(solution)/shard_map/ppermute | solution.py:18
  178.2 5.8 %collective-permute-start.26 = (f32[2,1024,8]{1,2,0:T(8,128)S(1)}, f32[2,1024,8]{1,2,0:T(8,128)S(1)}, u32[]{:S(2)}, u32[]{:S(2)}) collective-permute-start(f32[2,1024,8]{1,2,0:T(8,128)S(1)} %add_add_fusion.7), channel_id=1, source_target_pairs={{0,32},{4,36},{8,40},{12,44},{16,48},{20,52},{24,56},{28,60},{32,0... | collective-permute-start | bytes 196616 | tf_op jit(solution)/shard_map/ppermute | solution.py:18
  180.1 5.5 %collective-permute-start.27 = (f32[2,1024,8]{1,2,0:T(8,128)S(1)}, f32[2,1024,8]{1,2,0:T(8,128)S(1)}, u32[]{:S(2)}, u32[]{:S(2)}) collective-permute-start(f32[2,1024,8]{1,2,0:T(8,128)S(1)} %add_add_fusion.7), channel_id=1, source_target_pairs={{0,48},{4,52},{8,56},{12,60},{16,32},{20,36},{24,40},{28,44},{32,1... | collective-permute-start | bytes 196616 | tf_op jit(solution)/shard_map/ppermute | solution.py:18
  185.6 6.0 %collective-permute-start.28 = (f32[2,1024,8]{1,2,0:T(8,128)S(1)}, f32[2,1024,8]{1,2,0:T(8,128)S(1)}, u32[]{:S(2)}, u32[]{:S(2)}) collective-permute-start(f32[2,1024,8]{1,2,0:T(8,128)S(1)} %add_add_fusion.6), channel_id=1, source_target_pairs={{0,64},{4,68},{8,72},{12,76},{16,80},{20,84},{24,88},{28,92},{32,9... | collective-permute-start | bytes 196616 | tf_op jit(solution)/shard_map/ppermute | solution.py:18
  211.2 5.8 %collective-permute-start.30 = (f32[2,1024,8]{1,2,0:T(8,128)S(1)}, f32[2,1024,8]{1,2,0:T(8,128)S(1)}, u32[]{:S(2)}, u32[]{:S(2)}) collective-permute-start(f32[2,1024,8]{1,2,0:T(8,128)S(1)} %pad_maximum_fusion.4), channel_id=1, source_target_pairs={{0,8},{4,12},{8,0},{12,4},{16,24},{20,28},{24,16},{28,20},{32,40},... | collective-permute-start | bytes 196616 | tf_op jit(solution)/shard_map/ppermute | solution.py:18
  214.1 5.7 %collective-permute-start.31 = (f32[2,1024,8]{1,2,0:T(8,128)S(1)}, f32[2,1024,8]{1,2,0:T(8,128)S(1)}, u32[]{:S(2)}, u32[]{:S(2)}) collective-permute-start(f32[2,1024,8]{1,2,0:T(8,128)S(1)} %pad_maximum_fusion.4), channel_id=1, source_target_pairs={{0,12},{4,8},{8,4},{12,0},{16,28},{20,24},{24,20},{28,16},{32,44},... | collective-permute-start | bytes 196616 | tf_op jit(solution)/shard_map/ppermute | solution.py:18
  219.8 4.9 %collective-permute-start.32 = (f32[2,1024,8]{1,2,0:T(8,128)S(1)}, f32[2,1024,8]{1,2,0:T(8,128)S(1)}, u32[]{:S(2)}, u32[]{:S(2)}) collective-permute-start(f32[2,1024,8]{1,2,0:T(8,128)S(1)} %add_add_fusion.5), channel_id=1, source_target_pairs={{0,16},{4,20},{8,24},{12,28},{16,0},{20,4},{24,8},{28,12},{32,48},... | collective-permute-start | bytes 196616 | tf_op jit(solution)/shard_map/ppermute | solution.py:18
  220.6 6.8 %collective-permute-start.33 = (f32[2,1024,8]{1,2,0:T(8,128)S(1)}, f32[2,1024,8]{1,2,0:T(8,128)S(1)}, u32[]{:S(2)}, u32[]{:S(2)}) collective-permute-start(f32[2,1024,8]{1,2,0:T(8,128)S(1)} %add_add_fusion.5), channel_id=1, source_target_pairs={{0,32},{4,36},{8,40},{12,44},{16,48},{20,52},{24,56},{28,60},{32,0... | collective-permute-start | bytes 196616 | tf_op jit(solution)/shard_map/ppermute | solution.py:18
  224.0 5.5 %collective-permute-start.34 = (f32[2,1024,8]{1,2,0:T(8,128)S(1)}, f32[2,1024,8]{1,2,0:T(8,128)S(1)}, u32[]{:S(2)}, u32[]{:S(2)}) collective-permute-start(f32[2,1024,8]{1,2,0:T(8,128)S(1)} %add_add_fusion.5), channel_id=1, source_target_pairs={{0,48},{4,52},{8,56},{12,60},{16,32},{20,36},{24,40},{28,44},{32,1... | collective-permute-start | bytes 196616 | tf_op jit(solution)/shard_map/ppermute | solution.py:18
  229.5 6.1 %collective-permute-start.35 = (f32[2,1024,8]{1,2,0:T(8,128)S(1)}, f32[2,1024,8]{1,2,0:T(8,128)S(1)}, u32[]{:S(2)}, u32[]{:S(2)}) collective-permute-start(f32[2,1024,8]{1,2,0:T(8,128)S(1)} %add_add_fusion.4), channel_id=1, source_target_pairs={{0,64},{4,68},{8,72},{12,76},{16,80},{20,84},{24,88},{28,92},{32,9... | collective-permute-start | bytes 196616 | tf_op jit(solution)/shard_map/ppermute | solution.py:18
  255.0 4.8 %collective-permute-start.36 = (f32[2,1024,8]{1,2,0:T(8,128)S(1)}, f32[2,1024,8]{1,2,0:T(8,128)S(1)}, u32[]{:S(2)}, u32[]{:S(2)}) collective-permute-start(f32[2,1024,8]{1,2,0:T(8,128)S(1)} %pad_maximum_fusion.5), channel_id=1, source_target_pairs={{0,4},{4,0},{8,12},{12,8},{16,20},{20,16},{24,28},{28,24},{32,36},... | collective-permute-start | bytes 196616 | tf_op jit(solution)/shard_map/ppermute | solution.py:18
  255.1 6.1 %collective-permute-start.37 = (f32[2,1024,8]{1,2,0:T(8,128)S(1)}, f32[2,1024,8]{1,2,0:T(8,128)S(1)}, u32[]{:S(2)}, u32[]{:S(2)}) collective-permute-start(f32[2,1024,8]{1,2,0:T(8,128)S(1)} %pad_maximum_fusion.5), channel_id=1, source_target_pairs={{0,8},{4,12},{8,0},{12,4},{16,24},{20,28},{24,16},{28,20},{32,40},... | collective-permute-start | bytes 196616 | tf_op jit(solution)/shard_map/ppermute | solution.py:18
  258.3 5.5 %collective-permute-start.38 = (f32[2,1024,8]{1,2,0:T(8,128)S(1)}, f32[2,1024,8]{1,2,0:T(8,128)S(1)}, u32[]{:S(2)}, u32[]{:S(2)}) collective-permute-start(f32[2,1024,8]{1,2,0:T(8,128)S(1)} %pad_maximum_fusion.5), channel_id=1, source_target_pairs={{0,12},{4,8},{8,4},{12,0},{16,28},{20,24},{24,20},{28,16},{32,44},... | collective-permute-start | bytes 196616 | tf_op jit(solution)/shard_map/ppermute | solution.py:18
  263.9 5.8 %collective-permute-start.40 = (f32[2,1024,8]{1,2,0:T(8,128)S(1)}, f32[2,1024,8]{1,2,0:T(8,128)S(1)}, u32[]{:S(2)}, u32[]{:S(2)}) collective-permute-start(f32[2,1024,8]{1,2,0:T(8,128)S(1)} %add_add_fusion.3), channel_id=1, source_target_pairs={{0,32},{4,36},{8,40},{12,44},{16,48},{20,52},{24,56},{28,60},{32,0... | collective-permute-start | bytes 196616 | tf_op jit(solution)/shard_map/ppermute | solution.py:18
  266.1 5.5 %collective-permute-start.41 = (f32[2,1024,8]{1,2,0:T(8,128)S(1)}, f32[2,1024,8]{1,2,0:T(8,128)S(1)}, u32[]{:S(2)}, u32[]{:S(2)}) collective-permute-start(f32[2,1024,8]{1,2,0:T(8,128)S(1)} %add_add_fusion.3), channel_id=1, source_target_pairs={{0,48},{4,52},{8,56},{12,60},{16,32},{20,36},{24,40},{28,44},{32,1... | collective-permute-start | bytes 196616 | tf_op jit(solution)/shard_map/ppermute | solution.py:18
  271.5 6.1 %collective-permute-start.42 = (f32[2,1024,8]{1,2,0:T(8,128)S(1)}, f32[2,1024,8]{1,2,0:T(8,128)S(1)}, u32[]{:S(2)}, u32[]{:S(2)}) collective-permute-start(f32[2,1024,8]{1,2,0:T(8,128)S(1)} %add_add_fusion.2), channel_id=1, source_target_pairs={{0,64},{4,68},{8,72},{12,76},{16,80},{20,84},{24,88},{28,92},{32,9... | collective-permute-start | bytes 196616 | tf_op jit(solution)/shard_map/ppermute | solution.py:18
  297.2 6.1 %collective-permute-start.44 = (f32[2,1024,8]{1,2,0:T(8,128)S(1)}, f32[2,1024,8]{1,2,0:T(8,128)S(1)}, u32[]{:S(2)}, u32[]{:S(2)}) collective-permute-start(f32[2,1024,8]{1,2,0:T(8,128)S(1)} %pad_maximum_fusion.6), channel_id=1, source_target_pairs={{0,8},{4,12},{8,0},{12,4},{16,24},{20,28},{24,16},{28,20},{32,40},... | collective-permute-start | bytes 196616 | tf_op jit(solution)/shard_map/ppermute | solution.py:18
  300.4 5.5 %collective-permute-start.45 = (f32[2,1024,8]{1,2,0:T(8,128)S(1)}, f32[2,1024,8]{1,2,0:T(8,128)S(1)}, u32[]{:S(2)}, u32[]{:S(2)}) collective-permute-start(f32[2,1024,8]{1,2,0:T(8,128)S(1)} %pad_maximum_fusion.6), channel_id=1, source_target_pairs={{0,12},{4,8},{8,4},{12,0},{16,28},{20,24},{24,20},{28,16},{32,44},... | collective-permute-start | bytes 196616 | tf_op jit(solution)/shard_map/ppermute | solution.py:18
  306.0 6.7 %collective-permute-start.47 = (f32[2,1024,8]{1,2,0:T(8,128)S(1)}, f32[2,1024,8]{1,2,0:T(8,128)S(1)}, u32[]{:S(2)}, u32[]{:S(2)}) collective-permute-start(f32[2,1024,8]{1,2,0:T(8,128)S(1)} %add_add_fusion.1), channel_id=1, source_target_pairs={{0,32},{4,36},{8,40},{12,44},{16,48},{20,52},{24,56},{28,60},{32,0... | collective-permute-start | bytes 196616 | tf_op jit(solution)/shard_map/ppermute | solution.py:18
  309.7 5.5 %collective-permute-start.48 = (f32[2,1024,8]{1,2,0:T(8,128)S(1)}, f32[2,1024,8]{1,2,0:T(8,128)S(1)}, u32[]{:S(2)}, u32[]{:S(2)}) collective-permute-start(f32[2,1024,8]{1,2,0:T(8,128)S(1)} %add_add_fusion.1), channel_id=1, source_target_pairs={{0,48},{4,52},{8,56},{12,60},{16,32},{20,36},{24,40},{28,44},{32,1... | collective-permute-start | bytes 196616 | tf_op jit(solution)/shard_map/ppermute | solution.py:18
  315.2 6.1 %collective-permute-start.49 = (f32[2,1024,8]{1,2,0:T(8,128)S(1)}, f32[2,1024,8]{1,2,0:T(8,128)S(1)}, u32[]{:S(2)}, u32[]{:S(2)}) collective-permute-start(f32[2,1024,8]{1,2,0:T(8,128)S(1)} %add_add_fusion), channel_id=1, source_target_pairs={{0,64},{4,68},{8,72},{12,76},{16,80},{20,84},{24,88},{28,92},{32,9... | collective-permute-start | bytes 196616 | tf_op jit(solution)/shard_map/ppermute | solution.py:18
  346.9 5.2 %collective-permute-start.51 = (f32[16]{0:T(128)S(1)}, f32[16]{0:T(128)S(1)}, u32[]{:S(2)}, u32[]{:S(2)}) collective-permute-start(f32[16]{0:T(128)S(1)} %get-tuple-element.37), channel_id=1, source_target_pairs={{0,8},{4,12},{8,0},{12,4},{16,24},{20,28},{24,16},{28,20},{32,40},... | collective-permute-start | bytes 200 | tf_op jit(solution)/shard_map/ppermute | solution.py:18
  354.9 5.2 %collective-permute-start.54 = (f32[16]{0:T(128)S(1)}, f32[16]{0:T(128)S(1)}, u32[]{:S(2)}, u32[]{:S(2)}) collective-permute-start(f32[16]{0:T(128)S(1)} %add_add_fusion.15), channel_id=1, source_target_pairs={{0,32},{4,36},{8,40},{12,44},{16,48},{20,52},{24,56},{28,60},{32,0... | collective-permute-start | bytes 200 | tf_op jit(solution)/shard_map/ppermute | solution.py:18
  361.8 5.1 %collective-permute-start.56 = (f32[16]{0:T(128)S(1)}, f32[16]{0:T(128)S(1)}, u32[]{:S(2)}, u32[]{:S(2)}) collective-permute-start(f32[16]{0:T(128)S(1)} %add_add_fusion.14), channel_id=1, source_target_pairs={{0,64},{4,68},{8,72},{12,76},{16,80},{20,84},{24,88},{28,92},{32,9... | collective-permute-start | bytes 200 | tf_op jit(solution)/shard_map/ppermute | solution.py:18
  (18 other events, 192.9 us)
